TPU v7x, 32 devices: a whole 2x2x4 slice. The times are simulated.
32 devices in a mesh: member: 2 (over y), lon: 4 (over z), lev: 4 (over x, core).
Axes of the slice: x: 2, y: 2, z: 4, core: 2. Of those that a mesh axis runs over, the one named last changes fastest.
Arguments:
- latent: bfloat16 [512, 8, 512], P('lev', 'member', 'lon'), parts along dimension 1, may hold values from -9 to 9
- att_gain: float32 [512], replicated, may hold values from 0.1 to 1.9
- qkv_weight: bfloat16 [3, 512, 512], P(None, 'lev'), may hold values from -0.25 to 0.25
- out_weight: bfloat16 [512, 512], P('lev'), may hold values from -0.25 to 0.25
- stencil_weight: float32 [2, 9, 512], P(None, None, 'lev'), may hold values from -2.5 to 2.5
- block_gain: float32 [2, 512], replicated, may hold values from 0.1 to 1.9
- up_weight: bfloat16 [2, 2048, 512], P(None, 'lev'), may hold values from -0.25 to 0.25
- down_weight: bfloat16 [2, 2048, 512], P(None, 'lev'), may hold values from -0.125 to 0.125
Outputs:
- decoded: bfloat16 [512, 8, 512], P('lev', 'member', 'lon'), parts along dimension 1
There are 2 independent parts, one for each index of `member`. A program takes and returns all parts, laid end to end along the dimension named above; an argument that names none is the same for every part. Nothing has to cross between parts.
All inputs are finite; a program needn't handle non-finite values.
Results may differ from a plain program's by a relative error of at most 0.017.
Values may be sent and summed in bfloat16 or wider, within the bound.
No kernel may reach another device: no remote copies, remote signals or barrier semaphores. Data moves between devices by JAX's collectives and lax.ppermute only.
A program may use at most 64 MiB of HBM per device.

v0:
```python
import math
import jax
import jax.numpy as jnp
from jax import lax
from jax.sharding import PartitionSpec as P

C = 512
H = 8
BLOCKS = 2
attention_scale = 24.0
band_start = 30.0
grid_step = 0.25
epsilon = 1e-06


def secant_rows(count):
    rows = jnp.arange(count).astype(jnp.float32)
    return 1.0 / jnp.cos((band_start + grid_step * rows) * (math.pi / 180.0))


def norm_channels(values, gain):
    scale = lax.rsqrt(jnp.mean(values * values, axis=0, keepdims=True) + epsilon)
    return values * scale * gain[:, None, None]


def unit_heads(values):
    return values * lax.rsqrt(jnp.sum(values * values, axis=1, keepdims=True) + epsilon)


def gather_channels(values):
    return lax.all_gather(values, "lev", axis=0, tiled=True)


def scatter_sum(partial, axis):
    devices = lax.axis_size(axis)
    me = lax.axis_index(axis)
    chips, core = (devices // 2, me % 2)
    chip = me // 2
    blocks = partial.reshape(chips, 2, -1, *partial.shape[1:])
    mine = jnp.take(blocks, core, axis=1).astype(jnp.float32)
    theirs = jnp.take(blocks, 1 - core, axis=1)
    pair = mine + lax.ppermute(theirs, axis, [(i, i ^ 1) for i in range(devices)]).astype(
        jnp.float32
    )
    total = jnp.take(pair, chip, axis=0)
    for shift in range(1, chips):
        pairs = [(i, (i // 2 + shift) % chips * 2 + i % 2) for i in range(devices)]
        sent = jnp.take(pair, (chip + shift) % chips, axis=0).astype(jnp.bfloat16)
        total = total + lax.ppermute(sent, axis, pairs).astype(jnp.float32)
    return total


def spread_sum(weight, activation):
    partial = lax.dot_general(
        weight, activation, (((0,), (0,)), ((), ())), preferred_element_type=jnp.float32
    ).astype(jnp.bfloat16)
    return scatter_sum(partial, "lev")


def gather_strips(values, axis):
    devices = lax.axis_size(axis)
    pieces = [values]
    for shift in range(1, devices):
        pairs = [(i, (i + shift) % devices) for i in range(devices)]
        pieces.append(lax.ppermute(values, axis, pairs))
    return jnp.concatenate(pieces, axis=-1)


def make_fold(queries, pieces):
    key_part, value_part = pieces
    scores = (
        jnp.einsum("hdri,phdrj->hripj", queries, key_part, preferred_element_type=jnp.float32)
        * attention_scale
    )
    weights = jnp.exp(scores)
    numerator = jnp.einsum(
        "hripj,phdrj->hdri",
        weights.astype(jnp.bfloat16),
        value_part,
        preferred_element_type=jnp.float32,
    )
    return (numerator, jnp.sum(weights, axis=(3, 4)))


def block_apply(state, block_index, stencil_weight, block_gain, up_weight, down_weight):
    lat_rows = state.shape[1]
    out_cols = state.shape[2] - 2
    secants = secant_rows(lat_rows)[None, :, None]
    padded = jnp.pad(state.astype(jnp.float32), ((0, 0), (1, 1), (0, 0)))
    tap_weights = stencil_weight[block_index]
    stencil_sum = jnp.zeros((state.shape[0], lat_rows, out_cols), jnp.float32)
    for row_step in (-1, 0, 1):
        for col_step in (-1, 0, 1):
            shifted = padded[
                :, 1 + row_step : 1 + row_step + lat_rows, 1 + col_step : 1 + col_step + out_cols
            ]
            tap_row = tap_weights[3 * (row_step + 1) + col_step + 1][:, None, None]
            if col_step != 0:
                stencil_sum = stencil_sum + tap_row * secants * shifted
            else:
                stencil_sum = stencil_sum + tap_row * shifted
    smoothed = stencil_sum.astype(jnp.bfloat16)
    full_channels = gather_channels(smoothed.reshape(smoothed.shape[0], -1)).reshape(
        -1, *smoothed.shape[1:]
    )
    block_normed = norm_channels(full_channels.astype(jnp.float32), block_gain[block_index]).astype(
        jnp.bfloat16
    )
    block_normed = block_normed.reshape(full_channels.shape[0], -1)
    hidden = jax.nn.gelu(
        jnp.dot(up_weight[block_index], block_normed, preferred_element_type=jnp.float32)
    ).astype(jnp.bfloat16)
    update = spread_sum(down_weight[block_index], hidden)
    center = state[:, :, 1:-1]
    return (center.astype(jnp.float32) + update.reshape(center.shape)).astype(jnp.bfloat16)


def edges(values, width):
    return jnp.concatenate([values[..., :width], values[..., -width:]], axis=-1)


def per_device(
    latent, att_gain, qkv_weight, out_weight, stencil_weight, block_gain, up_weight, down_weight
):
    ch_local, lat_rows, columns = latent.shape
    head_size = C // H
    heads_local = qkv_weight.shape[1] // head_size
    reach = BLOCKS
    gathered = gather_channels(latent.reshape(ch_local, -1)).reshape(-1, lat_rows, columns)
    normed = norm_channels(gathered.astype(jnp.float32), att_gain).astype(jnp.bfloat16)
    projected = jnp.einsum("koc,crw->korw", qkv_weight, normed, preferred_element_type=jnp.float32)
    projected = projected.reshape(3, heads_local, head_size, lat_rows, columns)
    queries = unit_heads(projected[0]).astype(jnp.bfloat16)
    key_rows = unit_heads(projected[1]).astype(jnp.bfloat16)
    value_rows = projected[2].astype(jnp.bfloat16)
    key_value = jnp.stack([key_rows, value_rows]).reshape(-1, lat_rows, columns)
    rim = jnp.stack(
        [edges(queries.reshape(ch_local, lat_rows, columns), reach), edges(latent, reach)]
    )
    rim_rows = rim.size // (lat_rows * columns)
    payload = jnp.concatenate([key_value, rim.reshape(rim_rows, lat_rows, columns)], axis=0)
    strips = lax.axis_size("lon")
    pieces = [key_value]
    from_left = from_right = None
    for shift in range(1, strips):
        pairs = [(i, (i + shift) % strips) for i in range(strips)]
        sent = payload if shift in (1, strips - 1) else key_value
        got = lax.ppermute(sent, "lon", pairs)
        pieces.append(got[: key_value.shape[0]])
        if shift == 1:
            from_left = got[key_value.shape[0] :].reshape(rim.shape)[..., reach:]
        if shift == strips - 1:
            from_right = got[key_value.shape[0] :].reshape(rim.shape)[..., :reach]
    all_keys = jnp.stack(pieces).reshape(strips, 2, heads_local, head_size, lat_rows, columns)
    wide_queries = jnp.concatenate(
        [from_left[0], queries.reshape(ch_local, lat_rows, columns), from_right[0]], axis=-1
    ).reshape(heads_local, head_size, lat_rows, -1)
    wide_latent = jnp.concatenate([from_left[1], latent, from_right[1]], axis=-1)
    numerator, denominator = make_fold(wide_queries, (all_keys[:, 0], all_keys[:, 1]))
    attended = (numerator / denominator[:, None]).astype(jnp.bfloat16)
    update = spread_sum(out_weight, attended.reshape(ch_local, -1))
    current = (wide_latent.astype(jnp.float32) + update.reshape(wide_latent.shape)).astype(
        jnp.bfloat16
    )
    for block_index in range(BLOCKS):
        current = block_apply(
            current, block_index, stencil_weight, block_gain, up_weight, down_weight
        )
    return current


def solution(mesh):
    placed = (
        P("lev", "member", "lon"),
        P(),
        P(None, "lev", None),
        P("lev", None),
        P(None, None, "lev"),
        P(),
        P(None, "lev", None),
        P(None, "lev", None),
    )
    return jax.shard_map(
        per_device, mesh=mesh, in_specs=placed, out_specs=P("lev", "member", "lon"), check_vma=False
    )
```

profile of v0, /device:TPU:16, one launch (start us, length us, event | category | flops | bytes accessed | tf_op | source)
XLA Modules:
  0.0 84.5 jit_solution(3306220149589290437)
XLA Ops:
  0.0 1.1 %copy.88 = bf16[128,4,128]{0,2,1:T(8,128)(2,1)S(1)} copy(bf16[128,4,128]{2,1,0:T(4,128)(2,1)} %param.20) | data formatting | bytes 262144 | tf_op args[0]
  1.1 7.2 %all_gather.9 = bf16[512,512]{0,1:T(8,128)(2,1)S(1)} all-gather(bf16[128,512]{0,1:T(8,128)(2,1)S(1)} %bitcast.197), channel_id=1, replica_groups=mesh['member'=2,'lon'=4,'lev'=4] {'lev'}, dimensions={0}, use_global_device_ids=true | all-gather | bytes 655360 | tf_op jit(solution)/shard_map/all_gather | solution.py:31
  10.8 2.8 %collective-permute-start.1 = (bf16[264,4,128]{2,0,1:T(8,128)(2,1)S(1)}, bf16[264,4,128]{2,0,1:T(8,128)(2,1)S(1)}, u32[]{:S(2)}, u32[]{:S(2)}) collective-permute-start(bf16[264,4,128]{2,0,1:T(8,128)(2,1)S(1)} %pad_maximum_fusion.1), channel_id=1, source_target_pairs={{0,12},{4,0},{8,4},{12,8},{1,13},{5,1},{9,5},{13,9},{2,14},{6,2},{... | collective-permute-start | bytes 811016 | tf_op jit(solution)/shard_map/ppermute | solution.py:148
  13.7 19.3 %collective-permute-done.1 = bf16[264,4,128]{2,0,1:T(8,128)(2,1)S(1)} collective-permute-done((bf16[264,4,128]{2,0,1:T(8,128)(2,1)S(1)}, bf16[264,4,128]{2,0,1:T(8,128)(2,1)S(1)}, u32[]{:S(2)}, u32[]{:S(2)}) %collective-permute-start.1) | collective-permute-done | bytes 270368 | tf_op jit(solution)/shard_map/ppermute | solution.py:148
  33.0 0.6 reshape.631
  33.7 2.4 %collective-permute-done = bf16[264,4,128]{2,0,1:T(8,128)(2,1)S(1)} collective-permute-done((bf16[264,4,128]{2,0,1:T(8,128)(2,1)S(1)}, bf16[264,4,128]{2,0,1:T(8,128)(2,1)S(1)}, u32[]{:S(2)}, u32[]{:S(2)}) %collective-permute-start) | collective-permute-done | bytes 270368 | tf_op jit(solution)/shard_map/ppermute | solution.py:148
  36.1 0.6 reshape.630
  37.1 0.9 %fusion = (f32[2,4,132]{2,1,0:T(4,128)S(1)}, f32[2,4,132,4,128]{4,2,3,1,0:T(8,128)S(1)}) fusion(bf16[4,2,2,64,4,128]{5,3,0,4,2,1:T(8,128)(2,1)S(1)} %pad_maximum_fusion, bf16[2,64,4,2]{3,1,2,0:T(8,128)(2,1)S(1)} %copy.114, bf16[2,64,4,128]{3,1,2,0:T(8,128)(2,1)S(1)} %fusion.115, bf16[2,64,4,2]{3,1,2,0:T(8,128)(2,1)S(1)} %copy.113), kind=kOutput, calls=%fused_computation.1 | convolution fusion | flops 70691808 | bytes 3084416 | tf_op jit(solution)/shard_map/hdri,phdrj->hripj/dot_general | solution.py:72
  39.4 1.1 %constant_dynamic-slice_fusion.3 = (bf16[2,1,128,528]{2,1,0,3:T(2,128)(2,1)S(1)}, bf16[2,1,128,528]{2,1,0,3:T(2,128)(2,1)S(1)}) fusion(bf16[2,2,128,528]{2,1,0,3:T(2,128)(2,1)S(1)} %reshape.633, s32[]{:T(128)S(6)} %select_n.94, s32[]{:T(128)S(6)} %select_n.96), kind=kLoop, calls=%fused_computation.173 | loop fusion | bytes 1081352 | tf_op jit(solution)/shard_map/jit(_take) | solution.py:40
  40.9 1.3 %collective-permute-done.3 = bf16[2,128,528]{1,2,0:T(8,128)(2,1)S(1)} collective-permute-done((bf16[2,128,528]{1,2,0:T(8,128)(2,1)S(1)}, bf16[2,128,528]{1,2,0:T(8,128)(2,1)S(1)}, u32[]{:S(2)}, u32[]{:S(2)}) %collective-permute-start.3) | collective-permute-done | bytes 270368 | tf_op jit(solution)/shard_map/ppermute | solution.py:42
  42.3 1.2 %collective-permute-start.4 = (bf16[128,528]{0,1:T(8,128)(2,1)S(1)}, bf16[128,528]{0,1:T(8,128)(2,1)S(1)}, u32[]{:S(2)}, u32[]{:S(2)}) collective-permute-start(bf16[128,528]{0,1:T(8,128)(2,1)S(1)} %bitcast_convert_fusion), channel_id=1, source_target_pairs={{0,2},{1,3},{2,0},{3,1},{4,6},{5,7},{6,4},{7,5},{8,10},{9,11},{10,... | collective-permute-start | bytes 405512 | tf_op jit(solution)/shard_map/ppermute | solution.py:49
  43.7 4.3 %collective-permute-done.4 = bf16[128,528]{0,1:T(8,128)(2,1)S(1)} collective-permute-done((bf16[128,528]{0,1:T(8,128)(2,1)S(1)}, bf16[128,528]{0,1:T(8,128)(2,1)S(1)}, u32[]{:S(2)}, u32[]{:S(2)}) %collective-permute-start.4) | collective-permute-done | bytes 135200 | tf_op jit(solution)/shard_map/ppermute | solution.py:49
  48.4 7.0 %all_gather.10 = bf16[512,520]{0,1:T(8,128)(2,1)S(1)} all-gather(bf16[128,520]{0,1:T(8,128)(2,1)S(1)} %reshape.635), channel_id=1, replica_groups=mesh['member'=2,'lon'=4,'lev'=4] {'lev'}, dimensions={0}, use_global_device_ids=true | all-gather | bytes 665600 | tf_op jit(solution)/shard_map/all_gather | solution.py:31
  55.6 2.1 %fusion.3 = bf16[512,520]{0,1:T(8,128)(2,1)S(1)} fusion(bf16[512,520]{0,1:T(8,128)(2,1)S(1)} %all_gather.10, f32[512]{0:T(512)S(1)} %bitcast.213, f32[520]{0:T(1024)S(1)} %add_rsqrt_fusion, bf16[2,512,512]{2,1,0:T(8,128)(2,1)S(1)} %copy-done.5, bf16[2,512,512]{2,1,0:T(8,128)(2,1)} %param.26), kind=kOutput, calls=%fused_computation.16 | convolution fusion | flops 548986880 | bytes 2119680 | tf_op jit(solution)/shard_map/dot_general | solution.py:54
  57.8 1.1 %constant_dynamic-slice_fusion.1 = (bf16[2,1,128,520]{2,1,0,3:T(2,128)(2,1)S(1)}, bf16[2,1,128,520]{2,1,0,3:T(2,128)(2,1)S(1)}) fusion(bf16[2,2,128,520]{2,1,0,3:T(2,128)(2,1)S(1)} %reshape.636, s32[]{:T(128)S(6)} %select_n.94, s32[]{:T(128)S(6)} %select_n.96), kind=kLoop, calls=%fused_computation.171 | loop fusion | bytes 1064968 | tf_op jit(solution)/shard_map/jit(_take) | solution.py:40
  59.4 1.2 %collective-permute-done.5 = bf16[2,128,520]{1,2,0:T(8,128)(2,1)S(1)} collective-permute-done((bf16[2,128,520]{1,2,0:T(8,128)(2,1)S(1)}, bf16[2,128,520]{1,2,0:T(8,128)(2,1)S(1)}, u32[]{:S(2)}, u32[]{:S(2)}) %collective-permute-start.5) | collective-permute-done | bytes 266272 | tf_op jit(solution)/shard_map/ppermute | solution.py:42
  60.7 1.0 %collective-permute-start.6 = (bf16[128,520]{0,1:T(8,128)(2,1)S(1)}, bf16[128,520]{0,1:T(8,128)(2,1)S(1)}, u32[]{:S(2)}, u32[]{:S(2)}) collective-permute-start(bf16[128,520]{0,1:T(8,128)(2,1)S(1)} %bitcast_convert_fusion.1), channel_id=1, source_target_pairs={{0,2},{1,3},{2,0},{3,1},{4,6},{5,7},{6,4},{7,5},{8,10},{9,11},{10,... | collective-permute-start | bytes 399368 | tf_op jit(solution)/shard_map/ppermute | solution.py:49
  61.7 4.9 %collective-permute-done.6 = bf16[128,520]{0,1:T(8,128)(2,1)S(1)} collective-permute-done((bf16[128,520]{0,1:T(8,128)(2,1)S(1)}, bf16[128,520]{0,1:T(8,128)(2,1)S(1)}, u32[]{:S(2)}, u32[]{:S(2)}) %collective-permute-start.6) | collective-permute-done | bytes 133152 | tf_op jit(solution)/shard_map/ppermute | solution.py:49
  66.9 6.6 %all_gather.11 = bf16[512,512]{0,1:T(8,128)(2,1)S(1)} all-gather(bf16[128,512]{0,1:T(8,128)(2,1)S(1)} %bitcast.205), channel_id=1, replica_groups=mesh['member'=2,'lon'=4,'lev'=4] {'lev'}, dimensions={0}, use_global_device_ids=true | all-gather | bytes 655360 | tf_op jit(solution)/shard_map/all_gather | solution.py:31
  73.7 2.1 %convolution_convert_fusion.2 = bf16[512,512]{0,1:T(8,128)(2,1)S(1)} fusion(bf16[512,512]{0,1:T(8,128)(2,1)S(1)} %all_gather.11, bf16[2,512,512]{2,1,0:T(8,128)(2,1)S(1)} %copy-done.5, bf16[2,512,512]{2,1,0:T(8,128)(2,1)} %param.26, f32[512]{0:T(512)S(1)} %bitcast.212, f32[512]{0:T(512)S(1)} %add_rsqrt_fusion.1), kind=kOutput, calls=%fused_computation.13 | convolution fusion | flops 540540928 | bytes 2101248 | tf_op jit(solution)/shard_map/dot_general | solution.py:54
  76.3 1.2 %collective-permute-done.7 = bf16[2,128,512]{2,1,0:T(8,128)(2,1)S(1)} collective-permute-done((bf16[2,128,512]{2,1,0:T(8,128)(2,1)S(1)}, bf16[2,128,512]{2,1,0:T(8,128)(2,1)S(1)}, u32[]{:S(2)}, u32[]{:S(2)}) %collective-permute-start.7) | collective-permute-done | bytes 262176 | tf_op jit(solution)/shard_map/ppermute | solution.py:42
  77.6 1.2 %collective-permute-start.8 = (bf16[128,512]{1,0:T(8,128)(2,1)S(1)}, bf16[128,512]{1,0:T(8,128)(2,1)S(1)}, u32[]{:S(2)}, u32[]{:S(2)}) collective-permute-start(bf16[128,512]{1,0:T(8,128)(2,1)S(1)} %bitcast_convert_fusion.2), channel_id=1, source_target_pairs={{0,2},{1,3},{2,0},{3,1},{4,6},{5,7},{6,4},{7,5},{8,10},{9,11},{10,... | collective-permute-start | bytes 393224 | tf_op jit(solution)/shard_map/ppermute | solution.py:49
  78.8 4.6 %collective-permute-done.8 = bf16[128,512]{1,0:T(8,128)(2,1)S(1)} collective-permute-done((bf16[128,512]{1,0:T(8,128)(2,1)S(1)}, bf16[128,512]{1,0:T(8,128)(2,1)S(1)}, u32[]{:S(2)}, u32[]{:S(2)}) %collective-permute-start.8) | collective-permute-done | bytes 131104 | tf_op jit(solution)/shard_map/ppermute | solution.py:49
  83.7 0.8 copy.122
  (91 shorter events, 7.4 us)
Async XLA Ops:
  0.0 8.5 %copy-start = (bf16[3,128,512]{2,1,0:T(8,128)(2,1)S(1)}, bf16[3,128,512]{2,1,0:T(8,128)(2,1)}, u32[]{:S(2)}) copy-start(bf16[3,128,512]{2,1,0:T(8,128)(2,1)} %param.22) | copy-start | bytes 1179652
  0.0 8.5 %copy-start.4 = (f32[512]{0:T(512)S(1)}, f32[512]{0:T(512)}, u32[]{:S(2)}) copy-start(f32[512]{0:T(512)} %param.21) | copy-start | bytes 6148
  9.3 27.7 %collective-permute-start.2 = (bf16[256,4,128]{2,0,1:T(8,128)(2,1)S(1)}, bf16[256,4,128]{2,0,1:T(8,128)(2,1)S(1)}, u32[]{:S(2)}, u32[]{:S(2)}) collective-permute-start(bf16[256,4,128]{2,0,1:T(8,128)(2,1)S(1)} %bitcast.200), channel_id=1, source_target_pairs={{0,8},{4,12},{8,0},{12,4},{1,9},{5,13},{9,1},{13,5},{2,10},{6,14},... | collective-permute-start | bytes 786440 | tf_op jit(solution)/shard_map/ppermute | solution.py:148
  9.8 3.8 %copy-start.2 = (f32[2,9,128]{2,0,1:T(2,128)S(1)}, f32[2,9,128]{2,0,1:T(2,128)}, u32[]{:S(2)}) copy-start(f32[2,9,128]{2,0,1:T(2,128)} %param.24) | copy-start | bytes 27652
  10.8 22.2 %collective-permute-start.1 = (bf16[264,4,128]{2,0,1:T(8,128)(2,1)S(1)}, bf16[264,4,128]{2,0,1:T(8,128)(2,1)S(1)}, u32[]{:S(2)}, u32[]{:S(2)}) collective-permute-start(bf16[264,4,128]{2,0,1:T(8,128)(2,1)S(1)} %pad_maximum_fusion.1), channel_id=1, source_target_pairs={{0,12},{4,0},{8,4},{12,8},{1,13},{5,1},{9,5},{13,9},{2,14},{6,2},{... | collective-permute-start | bytes 811016 | tf_op jit(solution)/shard_map/ppermute | solution.py:148
  13.6 22.5 %collective-permute-start = (bf16[264,4,128]{2,0,1:T(8,128)(2,1)S(1)}, bf16[264,4,128]{2,0,1:T(8,128)(2,1)S(1)}, u32[]{:S(2)}, u32[]{:S(2)}) collective-permute-start(bf16[264,4,128]{2,0,1:T(8,128)(2,1)S(1)} %pad_maximum_fusion.1), channel_id=1, source_target_pairs={{0,4},{4,8},{8,12},{12,0},{1,5},{5,9},{9,13},{13,1},{2,6},{6,10},{... | collective-permute-start | bytes 811016 | tf_op jit(solution)/shard_map/ppermute | solution.py:148
  38.0 1.0 %copy-start.1 = (bf16[128,512]{1,0:T(8,128)(2,1)S(1)}, bf16[128,512]{1,0:T(8,128)(2,1)}, u32[]{:S(2)}) copy-start(bf16[128,512]{1,0:T(8,128)(2,1)} %param.23) | copy-start | bytes 393220
  40.5 2.9 %copy-start.3 = (f32[2,512]{1,0:T(2,128)S(1)}, f32[2,512]{1,0:T(2,128)}, u32[]{:S(2)}) copy-start(f32[2,512]{1,0:T(2,128)} %param.25) | copy-start | bytes 12292
  40.6 1.6 %collective-permute-start.3 = (bf16[2,128,528]{1,2,0:T(8,128)(2,1)S(1)}, bf16[2,128,528]{1,2,0:T(8,128)(2,1)S(1)}, u32[]{:S(2)}, u32[]{:S(2)}) collective-permute-start(bf16[2,128,528]{1,2,0:T(8,128)(2,1)S(1)} %fusion.90), channel_id=1, source_target_pairs={{0,1},{1,0},{2,3},{3,2},{4,5},{5,4},{6,7},{7,6},{8,9},{9,8},{10,11... | collective-permute-start | bytes 811016 | tf_op jit(solution)/shard_map/ppermute | solution.py:42
  42.3 5.7 %collective-permute-start.4 = (bf16[128,528]{0,1:T(8,128)(2,1)S(1)}, bf16[128,528]{0,1:T(8,128)(2,1)S(1)}, u32[]{:S(2)}, u32[]{:S(2)}) collective-permute-start(bf16[128,528]{0,1:T(8,128)(2,1)S(1)} %bitcast_convert_fusion), channel_id=1, source_target_pairs={{0,2},{1,3},{2,0},{3,1},{4,6},{5,7},{6,4},{7,5},{8,10},{9,11},{10,... | collective-permute-start | bytes 405512 | tf_op jit(solution)/shard_map/ppermute | solution.py:49
  48.1 7.5 %copy-start.5 = (bf16[2,512,512]{2,1,0:T(8,128)(2,1)S(1)}, bf16[2,512,512]{2,1,0:T(8,128)(2,1)}, u32[]{:S(2)}) copy-start(bf16[2,512,512]{2,1,0:T(8,128)(2,1)} %param.27) | copy-start | bytes 3145732
  59.0 1.6 %collective-permute-start.5 = (bf16[2,128,520]{1,2,0:T(8,128)(2,1)S(1)}, bf16[2,128,520]{1,2,0:T(8,128)(2,1)S(1)}, u32[]{:S(2)}, u32[]{:S(2)}) collective-permute-start(bf16[2,128,520]{1,2,0:T(8,128)(2,1)S(1)} %fusion.92), channel_id=1, source_target_pairs={{0,1},{1,0},{2,3},{3,2},{4,5},{5,4},{6,7},{7,6},{8,9},{9,8},{10,11... | collective-permute-start | bytes 798728 | tf_op jit(solution)/shard_map/ppermute | solution.py:42
  60.7 5.9 %collective-permute-start.6 = (bf16[128,520]{0,1:T(8,128)(2,1)S(1)}, bf16[128,520]{0,1:T(8,128)(2,1)S(1)}, u32[]{:S(2)}, u32[]{:S(2)}) collective-permute-start(bf16[128,520]{0,1:T(8,128)(2,1)S(1)} %bitcast_convert_fusion.1), channel_id=1, source_target_pairs={{0,2},{1,3},{2,0},{3,1},{4,6},{5,7},{6,4},{7,5},{8,10},{9,11},{10,... | collective-permute-start | bytes 399368 | tf_op jit(solution)/shard_map/ppermute | solution.py:49
  75.9 1.6 %collective-permute-start.7 = (bf16[2,128,512]{2,1,0:T(8,128)(2,1)S(1)}, bf16[2,128,512]{2,1,0:T(8,128)(2,1)S(1)}, u32[]{:S(2)}, u32[]{:S(2)}) collective-permute-start(bf16[2,128,512]{2,1,0:T(8,128)(2,1)S(1)} %select_bitcast_fusion), channel_id=1, source_target_pairs={{0,1},{1,0},{2,3},{3,2},{4,5},{5,4},{6,7},{7,6},{8,9},{9,8},{10,11... | collective-permute-start | bytes 786440 | tf_op jit(solution)/shard_map/ppermute | solution.py:42
  77.6 5.8 %collective-permute-start.8 = (bf16[128,512]{1,0:T(8,128)(2,1)S(1)}, bf16[128,512]{1,0:T(8,128)(2,1)S(1)}, u32[]{:S(2)}, u32[]{:S(2)}) collective-permute-start(bf16[128,512]{1,0:T(8,128)(2,1)S(1)} %bitcast_convert_fusion.2), channel_id=1, source_target_pairs={{0,2},{1,3},{2,0},{3,1},{4,6},{5,7},{6,4},{7,5},{8,10},{9,11},{10,... | collective-permute-start | bytes 393224 | tf_op jit(solution)/shard_map/ppermute | solution.py:49
where the time goes:
time: 84.7 us; the launch traced here: 84.5 us
  waiting for transfers between devices  39.2 us (46%)
  blocking collectives  20.9 us (25%)
  local copies, waits for them, and re-layouts  7.75 us (9%)
  starting transfers between devices  7.44 us (9%)
  matrix products  6.41 us (8%)
  other arithmetic  2.24 us (3%)
    ppermute x3, waiting for transfers between devices, per_device(): got = lax.ppermute(sent, 'lon', pairs)  21.7 us
    all_gather x3, blocking collectives, gather_channels(): return lax.all_gather(values, 'lev', axis=0, tiled=True)  20.9 us
    ppermute x3, waiting for transfers between devices, scatter_sum(): total = total + lax.ppermute(sent, axis, pairs).astype(jnp.float32)  13.8 us
    dot_general x3, matrix products, spread_sum(): lax.dot_general(weight, activation, (((0,), (0,)), ((), ())), preferred_e...  4.49 us
    ppermute x3, waiting for transfers between devices, scatter_sum(): lax.ppermute(theirs, axis, [(i, i ^ 1) for i in range(devices)])  3.69 us
    ppermute x3, starting transfers between devices, scatter_sum(): total = total + lax.ppermute(sent, axis, pairs).astype(jnp.float32)  3.34 us
    ppermute x3, starting transfers between devices, per_device(): got = lax.ppermute(sent, 'lon', pairs)  3.16 us
    another operation x2, local copies, waits for them, and re-layouts, scatter_sum(): mine = jnp.take(blocks, core, axis=1).astype(jnp.float32)  2.23 us
  transfers between devices with their start and end apart: 9, of which 8 were waited for; matrix products, arithmetic and copies ran while one was open for 4% of the time, Pallas kernels for 0%

commit v1 on v0

--- a/solution.py
+++ b/solution.py
@@ -13,6 +13,13 @@
 epsilon = 1e-06
 
 
+def read_the_tasks(body, axis_no):
+    y1 = list(body.shape[1:])
+    y1[axis_no] *= body.shape[0]
+    val2 = jnp.moveaxis(body, 0, axis_no).reshape(y1)
+    return val2
+
+
 def secant_rows(count):
     rows = jnp.arange(count).astype(jnp.float32)
     return 1.0 / jnp.cos((band_start + grid_step * rows) * (math.pi / 180.0))
@@ -28,7 +35,27 @@
 
 
 def gather_channels(values):
-    return lax.all_gather(values, "lev", axis=0, tiled=True)
+
+    def put_series_all(frame, row_axis, out_dim=0):
+        extent = jax.lax.axis_size(row_axis)
+        by_rank = [(no, (no + 1) % extent) for no in range(extent)]
+        chunks = [(dd, tick) for tick, dd in by_rank]
+        carry, base_arr = ([], [])
+        for h in tuple(range(extent - 1)):
+            if h % 2 == 0:
+                carry.append(jax.lax.ppermute(carry[-1] if carry else frame, row_axis, by_rank))
+            else:
+                response = jax.lax.ppermute(base_arr[-1] if base_arr else frame, row_axis, chunks)
+                base_arr.append(response)
+        opened = jnp.stack([*carry[::-1], frame, *base_arr], axis=0)
+        arr_next = jax.lax.axis_index(row_axis)
+        z2 = len(carry)
+        moved = arr_next - z2
+        opened = opened[(jnp.arange(extent) - moved) % extent]
+        tall = read_the_tasks(opened, out_dim)
+        return tall
+
+    return put_series_all(values, "lev")
 
 
 def scatter_sum(partial, axis):

time: 84.7 us -> 97.7 us (1.15)
  the two profiles are of different devices: /device:TPU:16 before, /device:TPU:0 now
where the time goes in v1:
time: 97.7 us; the launch traced here: 97.4 us
  waiting for transfers between devices  62.1 us (64%)
  local copies, waits for them, and re-layouts  12.5 us (13%)
  starting transfers between devices  11.8 us (12%)
  matrix products  6.16 us (6%)
  other arithmetic  4.05 us (4%)
    ppermute x6, waiting for transfers between devices, put_series_all(): jax.lax.ppermute(carry[-1] if carry else frame, row_axis, by_rank)  22.6 us
    ppermute x3, waiting for transfers between devices, per_device(): got = lax.ppermute(sent, 'lon', pairs)  19.3 us
    ppermute x3, waiting for transfers between devices, scatter_sum(): total = total + lax.ppermute(sent, axis, pairs).astype(jnp.float32)  15.8 us
    ppermute x3, starting transfers between devices, put_series_all(): jax.lax.ppermute(base_arr[-1] if base_arr else frame, row_axis, chunks)  5.89 us
    ppermute x3, starting transfers between devices, per_device(): got = lax.ppermute(sent, 'lon', pairs)  4.73 us
    ppermute x3, waiting for transfers between devices, scatter_sum(): lax.ppermute(theirs, axis, [(i, i ^ 1) for i in range(devices)])  4.45 us
    dot_general x3, matrix products, spread_sum(): lax.dot_general(weight, activation, (((0,), (0,)), ((), ())), preferred_e...  4.36 us
    unnamed x15, local copies, waits for them, and re-layouts  2.56 us
  transfers between devices with their start and end apart: 18, of which 15 were waited for; matrix products, arithmetic and copies ran while one was open for 4% of the time, Pallas kernels for 0%

profile of v1, /device:TPU:0, one launch (start us, length us, event | category | flops | bytes accessed | tf_op | source)
XLA Modules:
  0.0 97.4 jit_solution(15247182305255891651)
XLA Ops:
  1.0 2.4 %collective-permute-start.2 = (bf16[128,512]{1,0:T(8,128)(2,1)S(1)}, bf16[128,512]{1,0:T(8,128)(2,1)S(1)}, u32[]{:S(2)}, u32[]{:S(2)}) collective-permute-start(bf16[128,512]{1,0:T(8,128)(2,1)S(1)} %bitcast.239), channel_id=1, source_target_pairs={{1,0},{2,1},{3,2},{0,3},{5,4},{6,5},{7,6},{4,7},{9,8},{10,9},{11,1... | collective-permute-start | bytes 393224 | tf_op jit(solution)/shard_map/ppermute | solution.py:48
  4.5 3.9 %collective-permute-done = bf16[128,512]{1,0:T(8,128)(2,1)S(1)} collective-permute-done((bf16[128,512]{1,0:T(8,128)(2,1)S(1)}, bf16[128,512]{1,0:T(8,128)(2,1)S(1)}, u32[]{:S(2)}, u32[]{:S(2)}) %collective-permute-start) | collective-permute-done | bytes 131104 | tf_op jit(solution)/shard_map/ppermute | solution.py:46
  9.3 3.4 %collective-permute-done.1 = bf16[128,512]{1,0:T(8,128)(2,1)S(1)} collective-permute-done((bf16[128,512]{1,0:T(8,128)(2,1)S(1)}, bf16[128,512]{1,0:T(8,128)(2,1)S(1)}, u32[]{:S(2)}, u32[]{:S(2)}) %collective-permute-start.1) | collective-permute-done | bytes 131104 | tf_op jit(solution)/shard_map/ppermute | solution.py:46
  14.1 1.5 %fusion.46 = bf16[512,4,128,1]{2,1,0,3:T(4,128)(2,1)S(1)} fusion(f32[512,4,128]{2,1,0:T(4,128)S(1)} %reshape.1035, f32[512]{0:T(512)S(1)} %copy-done.4, f32[4,128]{1,0:T(4,128)S(1)} %rsqrt_bitcast_fusion), kind=kLoop, calls=%fused_computation.72 | loop fusion | flops 786432 | bytes 1576960 | tf_op jit(solution)/shard_map/convert_element_type | solution.py:157
  17.3 3.7 %collective-permute-start.4 = (bf16[264,4,128]{2,0,1:T(8,128)(2,1)S(1)}, bf16[264,4,128]{2,0,1:T(8,128)(2,1)S(1)}, u32[]{:S(2)}, u32[]{:S(2)}) collective-permute-start(bf16[264,4,128]{2,0,1:T(8,128)(2,1)S(1)} %pad_maximum_fusion.4), channel_id=1, source_target_pairs={{0,12},{4,0},{8,4},{12,8},{1,13},{5,1},{9,5},{13,9},{2,14},{6,2},{... | collective-permute-start | bytes 811016 | tf_op jit(solution)/shard_map/ppermute | solution.py:175
  22.1 5.8 %collective-permute-done.4 = bf16[264,4,128]{2,0,1:T(8,128)(2,1)S(1)} collective-permute-done((bf16[264,4,128]{2,0,1:T(8,128)(2,1)S(1)}, bf16[264,4,128]{2,0,1:T(8,128)(2,1)S(1)}, u32[]{:S(2)}, u32[]{:S(2)}) %collective-permute-start.4) | collective-permute-done | bytes 270368 | tf_op jit(solution)/shard_map/ppermute | solution.py:175
  28.6 6.1 %collective-permute-done.3 = bf16[264,4,128]{2,0,1:T(8,128)(2,1)S(1)} collective-permute-done((bf16[264,4,128]{2,0,1:T(8,128)(2,1)S(1)}, bf16[264,4,128]{2,0,1:T(8,128)(2,1)S(1)}, u32[]{:S(2)}, u32[]{:S(2)}) %collective-permute-start.3) | collective-permute-done | bytes 270368 | tf_op jit(solution)/shard_map/ppermute | solution.py:175
  35.6 7.3 %collective-permute-done.5 = bf16[256,4,128]{2,0,1:T(8,128)(2,1)S(1)} collective-permute-done((bf16[256,4,128]{2,0,1:T(8,128)(2,1)S(1)}, bf16[256,4,128]{2,0,1:T(8,128)(2,1)S(1)}, u32[]{:S(2)}, u32[]{:S(2)}) %collective-permute-start.5) | collective-permute-done | bytes 262176 | tf_op jit(solution)/shard_map/ppermute | solution.py:175
  45.3 1.1 %constant_dynamic-slice_fusion.3 = (bf16[2,1,128,528]{2,1,0,3:T(2,128)(2,1)S(1)}, bf16[2,1,128,528]{2,1,0,3:T(2,128)(2,1)S(1)}) fusion(bf16[2,2,128,528]{2,1,0,3:T(2,128)(2,1)S(1)} %reshape.781, s32[]{:T(128)S(6)} %select_n.125, s32[]{:T(128)S(6)} %select_n.127), kind=kLoop, calls=%fused_computation.179 | loop fusion | bytes 1081352 | tf_op jit(solution)/shard_map/jit(_take) | solution.py:67
  46.7 1.4 %collective-permute-done.6 = bf16[2,128,528]{1,2,0:T(8,128)(2,1)S(1)} collective-permute-done((bf16[2,128,528]{1,2,0:T(8,128)(2,1)S(1)}, bf16[2,128,528]{1,2,0:T(8,128)(2,1)S(1)}, u32[]{:S(2)}, u32[]{:S(2)}) %collective-permute-start.6) | collective-permute-done | bytes 270368 | tf_op jit(solution)/shard_map/ppermute | solution.py:69
  49.2 4.7 %collective-permute-done.7 = bf16[128,528]{0,1:T(8,128)(2,1)S(1)} collective-permute-done((bf16[128,528]{0,1:T(8,128)(2,1)S(1)}, bf16[128,528]{0,1:T(8,128)(2,1)S(1)}, u32[]{:S(2)}, u32[]{:S(2)}) %collective-permute-start.7) | collective-permute-done | bytes 135200 | tf_op jit(solution)/shard_map/ppermute | solution.py:76
  54.4 1.7 %collective-permute-start.10 = (bf16[128,520]{0,1:T(8,128)(2,1)S(1)}, bf16[128,520]{0,1:T(8,128)(2,1)S(1)}, u32[]{:S(2)}, u32[]{:S(2)}) collective-permute-start(bf16[128,520]{0,1:T(8,128)(2,1)S(1)} %reshape.783), channel_id=1, source_target_pairs={{1,0},{2,1},{3,2},{0,3},{5,4},{6,5},{7,6},{4,7},{9,8},{10,9},{11,1... | collective-permute-start | bytes 399368 | tf_op jit(solution)/shard_map/ppermute | solution.py:48
  56.1 3.2 %collective-permute-done.8 = bf16[128,520]{0,1:T(8,128)(2,1)S(1)} collective-permute-done((bf16[128,520]{0,1:T(8,128)(2,1)S(1)}, bf16[128,520]{0,1:T(8,128)(2,1)S(1)}, u32[]{:S(2)}, u32[]{:S(2)}) %collective-permute-start.8) | collective-permute-done | bytes 133152 | tf_op jit(solution)/shard_map/ppermute | solution.py:46
  59.4 4.3 %collective-permute-done.9 = bf16[128,520]{0,1:T(8,128)(2,1)S(1)} collective-permute-done((bf16[128,520]{0,1:T(8,128)(2,1)S(1)}, bf16[128,520]{0,1:T(8,128)(2,1)S(1)}, u32[]{:S(2)}, u32[]{:S(2)}) %collective-permute-start.9) | collective-permute-done | bytes 133152 | tf_op jit(solution)/shard_map/ppermute | solution.py:46
  65.1 2.0 %fusion.3 = bf16[512,520]{0,1:T(8,128)(2,1)S(1)} fusion(bf16[2,512,512]{2,1,0:T(8,128)(2,1)S(1)} %copy-done.5, bf16[2,512,512]{2,1,0:T(8,128)(2,1)} %param.26, bf16[4,128,520]{1,2,0:T(8,128)(2,1)S(1)} %gather_fusion.1, f32[4,128]{1,0:T(4,128)S(1)} %bitcast.248, f32[520]{0:T(1024)S(1)} %add_rsqrt_fusion), kind=kOutput, calls=%fused_computation.19 | convolution fusion | flops 548986880 | bytes 2119680 | tf_op jit(solution)/shard_map/dot_general | solution.py:81
  67.3 1.1 %constant_dynamic-slice_fusion.1 = (bf16[2,1,128,520]{2,1,0,3:T(2,128)(2,1)S(1)}, bf16[2,1,128,520]{2,1,0,3:T(2,128)(2,1)S(1)}) fusion(bf16[2,2,128,520]{2,1,0,3:T(2,128)(2,1)S(1)} %reshape.784, s32[]{:T(128)S(6)} %select_n.125, s32[]{:T(128)S(6)} %select_n.127), kind=kLoop, calls=%fused_computation.177 | loop fusion | bytes 1064968 | tf_op jit(solution)/shard_map/jit(_take) | solution.py:67
  68.5 1.5 %collective-permute-done.11 = bf16[2,128,520]{1,2,0:T(8,128)(2,1)S(1)} collective-permute-done((bf16[2,128,520]{1,2,0:T(8,128)(2,1)S(1)}, bf16[2,128,520]{1,2,0:T(8,128)(2,1)S(1)}, u32[]{:S(2)}, u32[]{:S(2)}) %collective-permute-start.11) | collective-permute-done | bytes 266272 | tf_op jit(solution)/shard_map/ppermute | solution.py:69
  70.2 5.6 %collective-permute-done.12 = bf16[128,520]{0,1:T(8,128)(2,1)S(1)} collective-permute-done((bf16[128,520]{0,1:T(8,128)(2,1)S(1)}, bf16[128,520]{0,1:T(8,128)(2,1)S(1)}, u32[]{:S(2)}, u32[]{:S(2)}) %collective-permute-start.12) | collective-permute-done | bytes 133152 | tf_op jit(solution)/shard_map/ppermute | solution.py:76
  76.3 1.7 %collective-permute-start.15 = (bf16[128,512]{1,0:T(8,128)(2,1)S(1)}, bf16[128,512]{1,0:T(8,128)(2,1)S(1)}, u32[]{:S(2)}, u32[]{:S(2)}) collective-permute-start(bf16[128,512]{1,0:T(8,128)(2,1)S(1)} %copy.199), channel_id=1, source_target_pairs={{1,0},{2,1},{3,2},{0,3},{5,4},{6,5},{7,6},{4,7},{9,8},{10,9},{11,1... | collective-permute-start | bytes 393224 | tf_op jit(solution)/shard_map/ppermute | solution.py:48
  78.0 3.5 %collective-permute-done.13 = bf16[128,512]{1,0:T(8,128)(2,1)S(1)} collective-permute-done((bf16[128,512]{1,0:T(8,128)(2,1)S(1)}, bf16[128,512]{1,0:T(8,128)(2,1)S(1)}, u32[]{:S(2)}, u32[]{:S(2)}) %collective-permute-start.13) | collective-permute-done | bytes 131104 | tf_op jit(solution)/shard_map/ppermute | solution.py:46
  81.7 4.3 %collective-permute-done.14 = bf16[128,512]{1,0:T(8,128)(2,1)S(1)} collective-permute-done((bf16[128,512]{1,0:T(8,128)(2,1)S(1)}, bf16[128,512]{1,0:T(8,128)(2,1)S(1)}, u32[]{:S(2)}, u32[]{:S(2)}) %collective-permute-start.14) | collective-permute-done | bytes 131104 | tf_op jit(solution)/shard_map/ppermute | solution.py:46
  86.9 2.1 %convolution_convert_fusion.2 = bf16[512,512]{0,1:T(8,128)(2,1)S(1)} fusion(bf16[512,512]{1,0:T(8,128)(2,1)S(1)} %bitcast.231, bf16[2,512,512]{2,1,0:T(8,128)(2,1)S(1)} %copy-done.5, bf16[2,512,512]{2,1,0:T(8,128)(2,1)} %param.26), kind=kOutput, calls=%fused_computation.16 | convolution fusion | flops 539492352 | bytes 2097152 | tf_op jit(solution)/shard_map/dot_general | solution.py:81
  89.1 1.5 %collective-permute-done.16 = bf16[2,128,512]{2,1,0:T(8,128)(2,1)S(1)} collective-permute-done((bf16[2,128,512]{2,1,0:T(8,128)(2,1)S(1)}, bf16[2,128,512]{2,1,0:T(8,128)(2,1)S(1)}, u32[]{:S(2)}, u32[]{:S(2)}) %collective-permute-start.16) | collective-permute-done | bytes 262176 | tf_op jit(solution)/shard_map/ppermute | solution.py:69
  90.8 5.5 %collective-permute-done.17 = bf16[128,512]{1,0:T(8,128)(2,1)S(1)} collective-permute-done((bf16[128,512]{1,0:T(8,128)(2,1)S(1)}, bf16[128,512]{1,0:T(8,128)(2,1)S(1)}, u32[]{:S(2)}, u32[]{:S(2)}) %collective-permute-start.17) | collective-permute-done | bytes 131104 | tf_op jit(solution)/shard_map/ppermute | solution.py:76
  (122 shorter events, 17.2 us)
Async XLA Ops:
  0.0 15.6 %copy-start = (bf16[3,128,512]{2,1,0:T(8,128)(2,1)S(1)}, bf16[3,128,512]{2,1,0:T(8,128)(2,1)}, u32[]{:S(2)}) copy-start(bf16[3,128,512]{2,1,0:T(8,128)(2,1)} %param.22) | copy-start | bytes 1179652
  1.0 8.3 %collective-permute-start.2 = (bf16[128,512]{1,0:T(8,128)(2,1)S(1)}, bf16[128,512]{1,0:T(8,128)(2,1)S(1)}, u32[]{:S(2)}, u32[]{:S(2)}) collective-permute-start(bf16[128,512]{1,0:T(8,128)(2,1)S(1)} %bitcast.239), channel_id=1, source_target_pairs={{1,0},{2,1},{3,2},{0,3},{5,4},{6,5},{7,6},{4,7},{9,8},{10,9},{11,1... | collective-permute-start | bytes 393224 | tf_op jit(solution)/shard_map/ppermute | solution.py:48
  3.4 4.9 %collective-permute-start = (bf16[128,512]{1,0:T(8,128)(2,1)S(1)}, bf16[128,512]{1,0:T(8,128)(2,1)S(1)}, u32[]{:S(2)}, u32[]{:S(2)}) collective-permute-start(bf16[128,512]{1,0:T(8,128)(2,1)S(1)} %bitcast.240), channel_id=1, source_target_pairs={{0,1},{1,2},{2,3},{3,0},{4,5},{5,6},{6,7},{7,4},{8,9},{9,10},{10,1... | collective-permute-start | bytes 393224 | tf_op jit(solution)/shard_map/ppermute | solution.py:46
  8.3 4.4 %collective-permute-start.1 = (bf16[128,512]{1,0:T(8,128)(2,1)S(1)}, bf16[128,512]{1,0:T(8,128)(2,1)S(1)}, u32[]{:S(2)}, u32[]{:S(2)}) collective-permute-start(bf16[128,512]{1,0:T(8,128)(2,1)S(1)} %collective-permute-done), channel_id=1, source_target_pairs={{0,1},{1,2},{2,3},{3,0},{4,5},{5,6},{6,7},{7,4},{8,9},{9,10},{10,1... | collective-permute-start | bytes 393224 | tf_op jit(solution)/shard_map/ppermute | solution.py:46
  13.4 0.7 copy-start.4
  17.3 10.6 %collective-permute-start.4 = (bf16[264,4,128]{2,0,1:T(8,128)(2,1)S(1)}, bf16[264,4,128]{2,0,1:T(8,128)(2,1)S(1)}, u32[]{:S(2)}, u32[]{:S(2)}) collective-permute-start(bf16[264,4,128]{2,0,1:T(8,128)(2,1)S(1)} %pad_maximum_fusion.4), channel_id=1, source_target_pairs={{0,12},{4,0},{8,4},{12,8},{1,13},{5,1},{9,5},{13,9},{2,14},{6,2},{... | collective-permute-start | bytes 811016 | tf_op jit(solution)/shard_map/ppermute | solution.py:175
  21.0 13.7 %collective-permute-start.3 = (bf16[264,4,128]{2,0,1:T(8,128)(2,1)S(1)}, bf16[264,4,128]{2,0,1:T(8,128)(2,1)S(1)}, u32[]{:S(2)}, u32[]{:S(2)}) collective-permute-start(bf16[264,4,128]{2,0,1:T(8,128)(2,1)S(1)} %pad_maximum_fusion.4), channel_id=1, source_target_pairs={{0,4},{4,8},{8,12},{12,0},{1,5},{5,9},{9,13},{13,1},{2,6},{6,10},{... | collective-permute-start | bytes 811016 | tf_op jit(solution)/shard_map/ppermute | solution.py:175
  21.0 21.9 %collective-permute-start.5 = (bf16[256,4,128]{2,0,1:T(8,128)(2,1)S(1)}, bf16[256,4,128]{2,0,1:T(8,128)(2,1)S(1)}, u32[]{:S(2)}, u32[]{:S(2)}) collective-permute-start(bf16[256,4,128]{2,0,1:T(8,128)(2,1)S(1)} %bitcast.225), channel_id=1, source_target_pairs={{0,8},{4,12},{8,0},{12,4},{1,9},{5,13},{9,1},{13,5},{2,10},{6,14},... | collective-permute-start | bytes 786440 | tf_op jit(solution)/shard_map/ppermute | solution.py:175
  43.9 1.0 copy-start.1
  45.3 1.4 %copy-start.2 = (f32[2,9,128]{2,0,1:T(2,128)S(1)}, f32[2,9,128]{2,0,1:T(2,128)}, u32[]{:S(2)}) copy-start(f32[2,9,128]{2,0,1:T(2,128)} %param.24) | copy-start | bytes 27652
  46.5 1.6 %collective-permute-start.6 = (bf16[2,128,528]{1,2,0:T(8,128)(2,1)S(1)}, bf16[2,128,528]{1,2,0:T(8,128)(2,1)S(1)}, u32[]{:S(2)}, u32[]{:S(2)}) collective-permute-start(bf16[2,128,528]{1,2,0:T(8,128)(2,1)S(1)} %fusion.81), channel_id=1, source_target_pairs={{0,1},{1,0},{2,3},{3,2},{4,5},{5,4},{6,7},{7,6},{8,9},{9,8},{10,11... | collective-permute-start | bytes 811016 | tf_op jit(solution)/shard_map/ppermute | solution.py:69
  48.2 5.7 %collective-permute-start.7 = (bf16[128,528]{0,1:T(8,128)(2,1)S(1)}, bf16[128,528]{0,1:T(8,128)(2,1)S(1)}, u32[]{:S(2)}, u32[]{:S(2)}) collective-permute-start(bf16[128,528]{0,1:T(8,128)(2,1)S(1)} %bitcast_convert_fusion), channel_id=1, source_target_pairs={{0,2},{1,3},{2,0},{3,1},{4,6},{5,7},{6,4},{7,5},{8,10},{9,11},{10,... | collective-permute-start | bytes 405512 | tf_op jit(solution)/shard_map/ppermute | solution.py:76
  54.0 5.4 %copy-start.3 = (f32[2,512]{1,0:T(2,128)S(1)}, f32[2,512]{1,0:T(2,128)}, u32[]{:S(2)}) copy-start(f32[2,512]{1,0:T(2,128)} %param.25) | copy-start | bytes 12292
  54.3 5.0 %collective-permute-start.8 = (bf16[128,520]{0,1:T(8,128)(2,1)S(1)}, bf16[128,520]{0,1:T(8,128)(2,1)S(1)}, u32[]{:S(2)}, u32[]{:S(2)}) collective-permute-start(bf16[128,520]{0,1:T(8,128)(2,1)S(1)} %reshape.783), channel_id=1, source_target_pairs={{0,1},{1,2},{2,3},{3,0},{4,5},{5,6},{6,7},{7,4},{8,9},{9,10},{10,1... | collective-permute-start | bytes 399368 | tf_op jit(solution)/shard_map/ppermute | solution.py:46
  54.4 5.0 %collective-permute-start.10 = (bf16[128,520]{0,1:T(8,128)(2,1)S(1)}, bf16[128,520]{0,1:T(8,128)(2,1)S(1)}, u32[]{:S(2)}, u32[]{:S(2)}) collective-permute-start(bf16[128,520]{0,1:T(8,128)(2,1)S(1)} %reshape.783), channel_id=1, source_target_pairs={{1,0},{2,1},{3,2},{0,3},{5,4},{6,5},{7,6},{4,7},{9,8},{10,9},{11,1... | collective-permute-start | bytes 399368 | tf_op jit(solution)/shard_map/ppermute | solution.py:48
  59.4 4.4 %collective-permute-start.9 = (bf16[128,520]{0,1:T(8,128)(2,1)S(1)}, bf16[128,520]{0,1:T(8,128)(2,1)S(1)}, u32[]{:S(2)}, u32[]{:S(2)}) collective-permute-start(bf16[128,520]{0,1:T(8,128)(2,1)S(1)} %collective-permute-done.8), channel_id=1, source_target_pairs={{0,1},{1,2},{2,3},{3,0},{4,5},{5,6},{6,7},{7,4},{8,9},{9,10},{10,1... | collective-permute-start | bytes 399368 | tf_op jit(solution)/shard_map/ppermute | solution.py:46
  63.9 1.2 %copy-start.5 = (bf16[2,512,512]{2,1,0:T(8,128)(2,1)S(1)}, bf16[2,512,512]{2,1,0:T(8,128)(2,1)}, u32[]{:S(2)}) copy-start(bf16[2,512,512]{2,1,0:T(8,128)(2,1)} %param.27) | copy-start | bytes 3145732
  68.4 1.6 %collective-permute-start.11 = (bf16[2,128,520]{1,2,0:T(8,128)(2,1)S(1)}, bf16[2,128,520]{1,2,0:T(8,128)(2,1)S(1)}, u32[]{:S(2)}, u32[]{:S(2)}) collective-permute-start(bf16[2,128,520]{1,2,0:T(8,128)(2,1)S(1)} %fusion.83), channel_id=1, source_target_pairs={{0,1},{1,0},{2,3},{3,2},{4,5},{5,4},{6,7},{7,6},{8,9},{9,8},{10,11... | collective-permute-start | bytes 798728 | tf_op jit(solution)/shard_map/ppermute | solution.py:69
  70.2 5.6 %collective-permute-start.12 = (bf16[128,520]{0,1:T(8,128)(2,1)S(1)}, bf16[128,520]{0,1:T(8,128)(2,1)S(1)}, u32[]{:S(2)}, u32[]{:S(2)}) collective-permute-start(bf16[128,520]{0,1:T(8,128)(2,1)S(1)} %bitcast_convert_fusion.1), channel_id=1, source_target_pairs={{0,2},{1,3},{2,0},{3,1},{4,6},{5,7},{6,4},{7,5},{8,10},{9,11},{10,... | collective-permute-start | bytes 399368 | tf_op jit(solution)/shard_map/ppermute | solution.py:76
  76.2 5.3 %collective-permute-start.13 = (bf16[128,512]{1,0:T(8,128)(2,1)S(1)}, bf16[128,512]{1,0:T(8,128)(2,1)S(1)}, u32[]{:S(2)}, u32[]{:S(2)}) collective-permute-start(bf16[128,512]{1,0:T(8,128)(2,1)S(1)} %copy.199), channel_id=1, source_target_pairs={{0,1},{1,2},{2,3},{3,0},{4,5},{5,6},{6,7},{7,4},{8,9},{9,10},{10,1... | collective-permute-start | bytes 393224 | tf_op jit(solution)/shard_map/ppermute | solution.py:46
  76.3 5.4 %collective-permute-start.15 = (bf16[128,512]{1,0:T(8,128)(2,1)S(1)}, bf16[128,512]{1,0:T(8,128)(2,1)S(1)}, u32[]{:S(2)}, u32[]{:S(2)}) collective-permute-start(bf16[128,512]{1,0:T(8,128)(2,1)S(1)} %copy.199), channel_id=1, source_target_pairs={{1,0},{2,1},{3,2},{0,3},{5,4},{6,5},{7,6},{4,7},{9,8},{10,9},{11,1... | collective-permute-start | bytes 393224 | tf_op jit(solution)/shard_map/ppermute | solution.py:48
  81.5 4.4 %collective-permute-start.14 = (bf16[128,512]{1,0:T(8,128)(2,1)S(1)}, bf16[128,512]{1,0:T(8,128)(2,1)S(1)}, u32[]{:S(2)}, u32[]{:S(2)}) collective-permute-start(bf16[128,512]{1,0:T(8,128)(2,1)S(1)} %collective-permute-done.13), channel_id=1, source_target_pairs={{0,1},{1,2},{2,3},{3,0},{4,5},{5,6},{6,7},{7,4},{8,9},{9,10},{10,1... | collective-permute-start | bytes 393224 | tf_op jit(solution)/shard_map/ppermute | solution.py:46
  89.0 1.6 %collective-permute-start.16 = (bf16[2,128,512]{2,1,0:T(8,128)(2,1)S(1)}, bf16[2,128,512]{2,1,0:T(8,128)(2,1)S(1)}, u32[]{:S(2)}, u32[]{:S(2)}) collective-permute-start(bf16[2,128,512]{2,1,0:T(8,128)(2,1)S(1)} %select_bitcast_fusion), channel_id=1, source_target_pairs={{0,1},{1,0},{2,3},{3,2},{4,5},{5,4},{6,7},{7,6},{8,9},{9,8},{10,11... | collective-permute-start | bytes 786440 | tf_op jit(solution)/shard_map/ppermute | solution.py:69
  90.7 5.6 %collective-permute-start.17 = (bf16[128,512]{1,0:T(8,128)(2,1)S(1)}, bf16[128,512]{1,0:T(8,128)(2,1)S(1)}, u32[]{:S(2)}, u32[]{:S(2)}) collective-permute-start(bf16[128,512]{1,0:T(8,128)(2,1)S(1)} %bitcast_convert_fusion.2), channel_id=1, source_target_pairs={{0,2},{1,3},{2,0},{3,1},{4,6},{5,7},{6,4},{7,5},{8,10},{9,11},{10,... | collective-permute-start | bytes 393224 | tf_op jit(solution)/shard_map/ppermute | solution.py:76
